TPU v7x, 512 devices: a whole 4x8x8 slice. The times are simulated.
512 devices in a mesh: seg: 16 (over z, x_lo), tok: 32 (over x_hi, y, core).
Axes of the slice: x: 4 (x_hi: 2, x_lo: 2; x = x_hi * 2 + x_lo), y: 8, z: 8, core: 2. Of those that a mesh axis runs over, the one named last changes fastest.
Arguments:
- seg_queries: bfloat16 [16, 4096, 2048], P('seg', 'tok'), may hold values from -8 to 8
- seg_keys: bfloat16 [16, 4096, 512], P('seg', 'tok'), may hold values from -8 to 8
- seg_values: bfloat16 [16, 4096, 512], P('seg', 'tok'), may hold values from -8 to 8
- grad_out: bfloat16 [16, 4096, 2048], P('seg', 'tok'), may hold values from -6 to 6
- mem_init: float32 [256, 1024], P('tok'), may hold values from -6 to 6
- mem_query: bfloat16 [256, 512], P('tok'), may hold values from -8 to 8
- retention: float32 [16, 1024], P('seg'), may hold values from 0 to 1
- seg_len: int32 [16], replicated, may hold values from 1024 to 4096, as said below
- doc_start: int32 [16], replicated, may hold values from 0 to 1, as said below
Outputs:
- attended: bfloat16 [16, 4096, 2048], P('seg', 'tok')
- memory_in: float32 [16, 256, 1024], P('seg', 'tok')
- memory_grad: float32 [16, 256, 1024], P('seg', 'tok')
Inputs may be any that keep to these rules, and one draw needn't show every extreme that they name: `seg_len`: A segment is full unless it is the last one of its document; segment 0 is always full and the last segment is the last one of its document. `doc_start`: segment 0 begins a document and segment 1 never does; any later segment may.
All inputs are finite; a program needn't handle non-finite values.
Results may differ from a plain program's by a relative error of at most 0.009.
Values may be sent and summed in bfloat16 or wider, within the bound.
No kernel may reach another device: no remote copies, remote signals or barrier semaphores. Data moves between devices by JAX's collectives and lax.ppermute only.
A program may use at most 64 MiB of HBM per device.

v0:
```python
import math
import jax
import jax.numpy as jnp
from jax import lax
from jax.sharding import PartitionSpec as P

HD = 128
QH = 16
KVH = 4
loss_scale = 16.0
neg_fill = -1e30
norm_eps = 1e-06


def slot_norm(raw_rows):
    parts = raw_rows.reshape(raw_rows.shape[0], 2 * KVH, HD)
    multiplier = lax.rsqrt(jnp.mean(parts * parts, axis=-1, keepdims=True) + norm_eps)
    return (parts * multiplier).reshape(raw_rows.shape)


def softmax_step(row_top, row_total, scores, allowed):
    scores = jnp.where(allowed, scores, neg_fill)
    new_top = jnp.maximum(row_top, jnp.max(scores, axis=-1))
    weights = jnp.where(allowed, jnp.exp(scores - new_top[..., None]), 0.0)
    multiplier = jnp.exp(row_top - new_top)
    new_total = row_total * multiplier + jnp.sum(weights, axis=-1)
    return (new_top, new_total, weights.astype(jnp.bfloat16), multiplier)


def shards(
    seg_queries, seg_keys, seg_values, grad_out, mem_init, mem_query, retention, seg_len, doc_start
):
    tok_rows = seg_queries.shape[1]
    mem_rows = mem_query.shape[0]
    group_size = QH // KVH
    width_kv = KVH * HD
    seg_count = lax.axis_size("seg")
    seg_index = lax.axis_index("seg")
    tok_index = lax.axis_index("tok")
    length = seg_len[seg_index]
    score_scale = 1.0 / math.sqrt(HD)
    queries = seg_queries[0].reshape(tok_rows, KVH, group_size, HD)
    slot_queries = mem_query.reshape(mem_rows, KVH, HD)
    row_pos = tok_index * tok_rows + jnp.arange(tok_rows)
    kv_piece = lax.all_gather(
        jnp.concatenate([seg_keys[0], seg_values[0]], axis=1), "tok", axis=0, tiled=True
    )
    piece_rows = kv_piece.shape[0]
    key_piece = kv_piece[:, :width_kv].reshape(piece_rows, KVH, HD)
    value_piece = kv_piece[:, width_kv:].reshape(piece_rows, KVH, HD)
    live_keys = jnp.arange(piece_rows) < length
    slot_scores = (
        jnp.einsum("rgd,ugd->gru", slot_queries, key_piece, preferred_element_type=jnp.float32)
        * score_scale
    )
    slot_scores = jnp.where(live_keys, slot_scores, neg_fill)
    slot_top = jnp.max(slot_scores, axis=-1, keepdims=True)
    slot_exp = jnp.where(live_keys, jnp.exp(slot_scores - slot_top), 0.0)
    slot_denom = jnp.transpose(jnp.sum(slot_exp, axis=-1))[..., None]
    slot_weights = slot_exp.astype(jnp.bfloat16)
    slot_keys = jnp.einsum(
        "gru,ugd->rgd", slot_weights, key_piece, preferred_element_type=jnp.float32
    )
    slot_values = jnp.einsum(
        "gru,ugd->rgd", slot_weights, value_piece, preferred_element_type=jnp.float32
    )
    raw_slots = jnp.concatenate(
        [
            (slot_keys / slot_denom).reshape(mem_rows, width_kv),
            (slot_values / slot_denom).reshape(mem_rows, width_kv),
        ],
        axis=1,
    )
    written = slot_norm(raw_slots)
    ret_row = retention[0]
    following = doc_start[jnp.minimum(seg_index + 1, seg_count - 1)].astype(jnp.float32)
    keep_flag = jnp.where(seg_index == seg_count - 1, 1.0, 1.0 - following)
    decay_rate = keep_flag * ret_row
    carried = keep_flag * (1.0 - ret_row) * written + (1.0 - keep_flag) * mem_init
    chain_terms = lax.all_gather(
        jnp.concatenate([carried, decay_rate[None]], axis=0), "seg", axis=0, tiled=False
    )
    all_carried = chain_terms[:, :mem_rows]
    all_decay = chain_terms[:, mem_rows]
    memory_in = mem_init
    for step in range(seg_count - 1):
        following_memory = all_decay[step] * memory_in + all_carried[step]
        memory_in = jnp.where(step < seg_index, following_memory, memory_in)
    block_rows = math.gcd(piece_rows, 512)
    blocks = piece_rows // block_rows
    key_blocks = key_piece.reshape(blocks, block_rows, KVH, HD)
    value_blocks = value_piece.reshape(blocks, block_rows, KVH, HD)
    block_first = block_rows * jnp.arange(blocks)
    starting = (
        jnp.full((KVH, group_size, tok_rows), neg_fill, jnp.float32),
        jnp.zeros((KVH, group_size, tok_rows), jnp.float32),
        jnp.zeros((tok_rows, KVH, group_size, HD), jnp.float32),
    )

    def one_block(inner_state, inputs):
        key_block, value_block, block_start = inputs
        columns = block_start + jnp.arange(block_rows)
        causal = (columns[None, :] <= row_pos[:, None]) & (columns < length)[None, :]
        seg_scores = (
            jnp.einsum("tgjd,ugd->gjtu", queries, key_block, preferred_element_type=jnp.float32)
            * score_scale
        )
        seg_top, seg_total, seg_weights, seg_factor = softmax_step(
            inner_state[0], inner_state[1], seg_scores, causal
        )
        seg_acc = inner_state[2] * jnp.transpose(seg_factor, (2, 0, 1))[..., None] + jnp.einsum(
            "gjtu,ugd->tgjd", seg_weights, value_block, preferred_element_type=jnp.float32
        )
        return ((seg_top, seg_total, seg_acc), None)

    running, _ = lax.scan(one_block, starting, (key_blocks, value_blocks, block_first))
    memory_all = lax.all_gather(memory_in.astype(jnp.bfloat16), "tok", axis=0, tiled=True)
    mem_keys = memory_all[:, :width_kv].reshape(-1, KVH, HD)
    mem_vals = memory_all[:, width_kv:].reshape(-1, KVH, HD)
    mem_scores = (
        jnp.einsum("tgjd,mgd->gjtm", queries, mem_keys, preferred_element_type=jnp.float32)
        * score_scale
    )
    row_top = jnp.maximum(running[0], jnp.max(mem_scores, axis=-1))
    seg_factor = jnp.exp(running[0] - row_top)
    mem_weights = jnp.exp(mem_scores - row_top[..., None])
    row_total = running[1] * seg_factor + jnp.sum(mem_weights, axis=-1)
    weighted = running[2] * jnp.transpose(seg_factor, (2, 0, 1))[..., None] + jnp.einsum(
        "gjtm,mgd->tgjd",
        mem_weights.astype(jnp.bfloat16),
        mem_vals,
        preferred_element_type=jnp.float32,
    )
    att_rows = weighted / jnp.transpose(row_total, (2, 0, 1))[..., None]
    log_total = row_top + jnp.log(row_total)
    attended = att_rows.reshape(1, tok_rows, QH * HD).astype(jnp.bfloat16)
    valid_rows = (row_pos < length).astype(jnp.bfloat16)[:, None]
    cotangent = (grad_out[0] * valid_rows * loss_scale).reshape(tok_rows, KVH, group_size, HD)
    row_delta = jnp.einsum("tgjd,tgjd->gjt", cotangent.astype(jnp.float32), att_rows)
    mem_prob = jnp.exp(mem_scores - log_total[..., None])
    grad_prob = jnp.einsum(
        "tgjd,mgd->gjtm", cotangent, mem_vals, preferred_element_type=jnp.float32
    )
    grad_score = mem_prob * (grad_prob - row_delta[..., None])
    grad_vals = jnp.einsum(
        "gjtm,tgjd->mgd",
        mem_prob.astype(jnp.bfloat16),
        cotangent,
        preferred_element_type=jnp.float32,
    )
    grad_keys = (
        jnp.einsum(
            "gjtm,tgjd->mgd",
            grad_score.astype(jnp.bfloat16),
            queries,
            preferred_element_type=jnp.float32,
        )
        * score_scale
    )
    grad_slots = jnp.concatenate(
        [grad_keys.reshape(-1, width_kv), grad_vals.reshape(-1, width_kv)], axis=1
    )
    local_grad = lax.psum_scatter(grad_slots, "tok", scatter_dimension=0, tiled=True)
    all_local = lax.all_gather(local_grad, "seg", axis=0, tiled=False)
    memory_grad = all_local[seg_count - 1]
    for step in range(seg_count - 2, -1, -1):
        earlier_grad = all_local[step] + all_decay[step] * memory_grad
        memory_grad = jnp.where(step >= seg_index, earlier_grad, memory_grad)
    return (attended, memory_in[None], memory_grad[None])


def solution(mesh):
    placed = (
        P("seg", "tok", None),
        P("seg", "tok", None),
        P("seg", "tok", None),
        P("seg", "tok", None),
        P("tok", None),
        P("tok", None),
        P("seg", None),
        P(),
        P(),
    )
    return jax.shard_map(
        shards,
        mesh=mesh,
        in_specs=placed,
        out_specs=(P("seg", "tok", None), P("seg", "tok", None), P("seg", "tok", None)),
        check_vma=False,
    )
```

profile of v0, /device:TPU:16, one launch (start us, length us, event | category | flops | bytes accessed | tf_op | source)
XLA Modules:
  0.0 526.6 jit_solution(17086343867945131486)
XLA Ops:
  18.4 108.9 %all-gather.5.cloned.1.call-done = bf16[4096,1024]{0,1:T(8,128)(2,1)} async-done(((bf16[128,1024]{0,1:T(8,128)(2,1)}), bf16[4096,1024]{0,1:T(8,128)(2,1)}) %all-gather.5.cloned.1.call-update) | async-done | bytes 8388624 | tf_op jit(solution)/shard_map/all_gather | solution.py:45
  127.3 5.9 %fusion.131 = (bf16[4096,512]{0,1:T(8,128)(2,1)}, bf16[4096,512]{0,1:T(8,128)(2,1)}) fusion(bf16[4096,1024]{0,1:T(8,128)(2,1)} %all-gather.5.cloned.1.call-done), kind=kLoop, calls=%fused_computation.186 | loop fusion | bytes 16777216 | tf_op jit(solution)/shard_map/slice | solution.py:49
  141.3 41.0 %all-gather.2 = f32[16,9,1024]{2,1,0:T(8,128)S(1)} all-gather(f32[1,9,1024]{2,1,0:T(8,128)S(1)} %maximum_bitcast_fusion), channel_id=2, replica_groups=mesh['seg'=16,'tok'=32] {'seg'}, dimensions={0}, use_global_device_ids=true | all-gather | bytes 626688 | tf_op jit(solution)/shard_map/all_gather | solution.py:80
  183.1 40.3 %all_gather.21 = bf16[256,1024]{1,0:T(8,128)(2,1)S(1)} all-gather(bf16[8,1024]{1,0:T(8,128)(2,1)S(1)} %get-tuple-element.175), channel_id=1, replica_groups=mesh['seg'=16,'tok'=32] {'tok'}, dimensions={0}, use_global_device_ids=true | all-gather | bytes 540672 | tf_op jit(solution)/shard_map/all_gather | solution.py:117
  226.3 6.4 %copy.166 = bf16[64,8,8,512]{3,2,1,0:T(8,128)(2,1)} copy(bf16[64,8,8,512]{3,1,2,0:T(8,128)(2,1)} %bitcast.463) | data formatting | bytes 8388608
  232.7 7.9 %copy.118 = bf16[8,512,4,128]{3,1,2,0:T(8,128)(2,1)} copy(bf16[8,512,4,128]{1,0,3,2:T(8,128)(2,1)} %bitcast.464) | data formatting | bytes 8388608
  240.6 4.4 copy.167
  248.5 100.9 %while.15 = (s32[]{:T(128)}, f32[4,4,128]{2,1,0:T(4,128)S(1)}, f32[4,4,128]{2,1,0:T(4,128)S(1)}, f32[128,4,4,128]{0,3,2,1:T(8,128)}, s32[8]{0:T(128)S(1)}, /*ind...) while((s32[]{:T(128)}, f32[4,4,128]{2,1,0:T(4,128)S(1)}, ...), condition=%wide.region_3.4_spmd.clone, body=%wide.region_0.3_spmd.clone.sunk | while | flops 551433856 | bytes 33431024 | solution.py:116
  251.3 3.8 fusion.160
  255.1 4.7 fusion.164
  263.6 3.8 fusion.160
  267.4 5.0 fusion.164
  276.3 3.8 fusion.160
  280.1 5.0 fusion.164
  288.9 3.8 fusion.160
  292.7 5.0 fusion.164
  301.6 3.8 fusion.160
  305.4 5.0 fusion.164
  314.2 3.8 fusion.160
  318.0 5.0 fusion.164
  330.7 5.0 fusion.164
  343.3 5.0 fusion.164
  361.9 120.3 %reduce-scatter.2.cloned.1.call-done = f32[8,1024]{1,0:T(8,128)} async-done(((f32[256,1024]{1,0:T(8,128)}), f32[8,1024]{1,0:T(8,128)}) %reduce-scatter.2.cloned.1.call-update) | async-done | bytes 32784 | tf_op jit(solution)/shard_map/reduce_scatter | solution.py:163
  482.2 36.8 %all-gather.1 = f32[128,1024]{1,0:T(8,128)S(1)} all-gather(f32[8,1024]{1,0:T(8,128)} %reduce-scatter.2.cloned.1.call-done), channel_id=3, replica_groups=mesh['seg'=16,'tok'=32] {'seg'}, dimensions={0}, use_global_device_ids=true | all-gather | bytes 557056 | tf_op jit(solution)/shard_map/all_gather | solution.py:164
  (197 shorter events, 77.0 us)
Async XLA Ops:
  7.2 126.1 %copy-start = (bf16[8,512]{1,0:T(8,128)(2,1)S(1)}, bf16[8,512]{1,0:T(8,128)(2,1)}, u32[]{:S(2)}) copy-start(bf16[8,512]{1,0:T(8,128)(2,1)} %param.16) | copy-start | bytes 24580
  7.2 8.6 %copy-start.15 = (s32[16]{0:T(128)S(1)}, s32[16]{0:T(128)}, u32[]{:S(2)}) copy-start(s32[16]{0:T(128)} %param.18) | copy-start | bytes 196
  7.2 11.2 %copy-start.13 = (f32[1,1024]{1,0:T(1,128)S(1)}, f32[1,1024]{1,0:T(1,128)}, u32[]{:S(2)}) copy-start(f32[1,1024]{1,0:T(1,128)} %param.17) | copy-start | bytes 12292
  7.2 120.1 %all-gather.5.cloned.1.call-start = ((), (), s32[]{:S(2)}) async-start(), calls=%async_computation.1 | async-start | bytes 8650752 | tf_op jit(solution)/shard_map/all_gather | solution.py:45
  10.1 472.2 %reduce-scatter.2.cloned.1.call-start = ((), (), s32[]{:S(2)}) async-start(), calls=%async_computation.2 | async-start | bytes 1081344 | tf_op jit(solution)/shard_map/reduce_scatter | solution.py:163
  136.3 3.5 copy-start.2
  136.3 4.8 copy-start.6
  255.1 4.7 copy-start.1
  267.4 5.0 copy-start.1
  272.4 1.1 copy-start.17
  280.1 5.0 copy-start.1
  285.0 1.1 copy-start.17
  292.7 5.0 copy-start.1
  305.4 5.0 copy-start.1
  318.0 5.0 copy-start.1
  330.7 5.0 copy-start.1
  343.3 5.0 copy-start.1
  349.4 4.6 copy-start.3
  349.4 4.6 copy-start.14
  351.2 4.2 copy-start.5
  357.2 3.7 copy-start.4
  357.2 161.9 %copy-start.8 = (f32[1,1,1024]{2,1,0:T(1,128)S(1)}, f32[1,1,1024]{2,1,0:T(1,128)}, u32[]{:S(2)}) copy-start(f32[1,1,1024]{2,1,0:T(1,128)} %copy-done.7) | copy-start | bytes 12292
  357.2 161.9 %copy-start.10 = (f32[1,1,1024]{2,1,0:T(1,128)S(1)}, f32[1,1,1024]{2,1,0:T(1,128)}, u32[]{:S(2)}) copy-start(f32[1,1,1024]{2,1,0:T(1,128)} %copy-done.9) | copy-start | bytes 12292
  357.2 161.9 %copy-start.12 = (f32[1,1,1024]{2,1,0:T(1,128)S(1)}, f32[1,1,1024]{2,1,0:T(1,128)}, u32[]{:S(2)}) copy-start(f32[1,1,1024]{2,1,0:T(1,128)} %copy-done.11) | copy-start | bytes 12292
  (17 other events, 13.4 us)
Sparse Core Ops, SparseCore 0:
  11.7 115.5 all-gather.4
  360.9 121.2 reduce-scatter.1
where the time goes:
time: 528 us; the launch traced here: 527 us
  waiting for transfers between devices  229 us (43%)
  blocking collectives  118 us (22%)
  matrix products  85 us (16%)
  local copies, waits for them, and re-layouts  45.9 us (9%)
  other arithmetic  32.6 us (6%)
  between operations  15 us (3%)
    reduce_scatter x1, waiting for transfers between devices, shards(): lax.psum_scatter(grad_slots, 'tok', scatter_dimension=0, tiled=True)  120 us
    all_gather x1, waiting for transfers between devices, shards(): lax.all_gather(jnp.concatenate([seg_keys[0], seg_values[0]], axis=1), 'to...  109 us
    all_gather x1, blocking collectives, shards(): lax.all_gather(jnp.concatenate([carried, decay_rate[None]], axis=0), 'seg...  41 us
    all_gather x1, blocking collectives, shards(): lax.all_gather(memory_in.astype(jnp.bfloat16), 'tok', axis=0, tiled=True)  40.3 us
    dot_general x8, matrix products, one_block(): jnp.einsum('gjtu,ugd->tgjd', seg_weights, value_block, preferred_element_...  39.5 us
    all_gather x1, blocking collectives, shards(): all_local = lax.all_gather(local_grad, 'seg', axis=0, tiled=False)  36.8 us
    dot_general x8, matrix products, one_block(): jnp.einsum('tgjd,ugd->gjtu', queries, key_block, preferred_element_type=j...  30 us
    unnamed x40, local copies, waits for them, and re-layouts  27.7 us
  transfers between devices with their start and end apart: 2, of which 2 were waited for; matrix products, arithmetic and copies ran while one was open for 2% of the time, Pallas kernels for 0%

commit v1 on v0

--- a/solution.py
+++ b/solution.py
@@ -114,7 +114,10 @@
         return ((seg_top, seg_total, seg_acc), None)
 
     running, _ = lax.scan(one_block, starting, (key_blocks, value_blocks, block_first))
-    memory_all = lax.all_gather(memory_in.astype(jnp.bfloat16), "tok", axis=0, tiled=True)
+    original = memory_in.astype(jnp.bfloat16)
+    memory_all = jnp.concatenate(
+        lax.all_to_all(jnp.stack(lax.axis_size("tok") * [original], axis=0), "tok", 0, 0), axis=0
+    )
     mem_keys = memory_all[:, :width_kv].reshape(-1, KVH, HD)
     mem_vals = memory_all[:, width_kv:].reshape(-1, KVH, HD)
     mem_scores = (

time: 528 us -> 496 us (0.939)
  blocking collectives: 118 us -> 77.8 us
  starting transfers between devices: 0.08 us -> 9.19 us
    all_gather x1 -> x0, blocking collectives: 40.3 us -> none  [shards(): lax.all_gather(memory_in.astype(jnp.bfloat16), 'tok', axis=0, tiled=True)]
    all_to_all x0 -> x1, starting transfers between devices: none -> 9.11 us  [shards(): lax.all_to_all(jnp.stack(lax.axis_size('tok') * [original], axis=0), 'tok...]
    unnamed x40 -> x23, local copies, waits for them, and re-layouts: 27.7 us -> 26.9 us
  transfers between devices with their start and end apart: 2 -> 3, of which waited for: 2 -> 2; matrix products, arithmetic and copies ran while one was open for 2% -> 26% of each run, Pallas kernels for 0% -> 0%
where the time goes in v1:
time: 496 us; the launch traced here: 494 us
  waiting for transfers between devices  231 us (47%)
  matrix products  84.3 us (17%)
  blocking collectives  77.8 us (16%)
  local copies, waits for them, and re-layouts  45.9 us (9%)
  other arithmetic  30.6 us (6%)
  between operations  15 us (3%)
  starting transfers between devices  9.19 us (2%)
    reduce_scatter x1, waiting for transfers between devices, shards(): lax.psum_scatter(grad_slots, 'tok', scatter_dimension=0, tiled=True)  121 us
    all_gather x1, waiting for transfers between devices, shards(): lax.all_gather(jnp.concatenate([seg_keys[0], seg_values[0]], axis=1), 'to...  110 us
    all_gather x1, blocking collectives, shards(): lax.all_gather(jnp.concatenate([carried, decay_rate[None]], axis=0), 'seg...  41 us
    dot_general x8, matrix products, one_block(): jnp.einsum('gjtu,ugd->tgjd', seg_weights, value_block, preferred_element_...  39.4 us
    all_gather x1, blocking collectives, shards(): all_local = lax.all_gather(local_grad, 'seg', axis=0, tiled=False)  36.8 us
    dot_general x8, matrix products, one_block(): jnp.einsum('tgjd,ugd->gjtu', queries, key_block, preferred_element_type=j...  29.9 us
    unnamed x23, local copies, waits for them, and re-layouts  26.9 us
    lt x8, other arithmetic, one_block(): columns < length  10.1 us
  transfers between devices with their start and end apart: 3, of which 2 were waited for; matrix products, arithmetic and copies ran while one was open for 26% of the time, Pallas kernels for 0%

profile of v1, /device:TPU:16, one launch (start us, length us, event | category | flops | bytes accessed | tf_op | source)
XLA Modules:
  0.0 494.4 jit_solution(15992602428137717392)
XLA Ops:
  16.9 110.4 %all-gather.5.cloned.1.call-done = bf16[4096,1024]{0,1:T(8,128)(2,1)} async-done(((bf16[128,1024]{0,1:T(8,128)(2,1)}), bf16[4096,1024]{0,1:T(8,128)(2,1)}) %all-gather.5.cloned.1.call-update) | async-done | bytes 8388624 | tf_op jit(solution)/shard_map/all_gather | solution.py:45
  127.3 5.9 %fusion.131 = (bf16[4096,512]{0,1:T(8,128)(2,1)}, bf16[4096,512]{0,1:T(8,128)(2,1)}) fusion(bf16[4096,1024]{0,1:T(8,128)(2,1)} %all-gather.5.cloned.1.call-done), kind=kLoop, calls=%fused_computation.186 | loop fusion | bytes 16777216 | tf_op jit(solution)/shard_map/slice | solution.py:49
  141.2 41.0 %all-gather.2 = f32[16,9,1024]{2,1,0:T(8,128)S(1)} all-gather(f32[1,9,1024]{2,1,0:T(8,128)S(1)} %maximum_bitcast_fusion), channel_id=2, replica_groups=mesh['seg'=16,'tok'=32] {'seg'}, dimensions={0}, use_global_device_ids=true | all-gather | bytes 626688 | tf_op jit(solution)/shard_map/all_gather | solution.py:80
  183.8 9.1 %all-to-all-start = ((bf16[32,8,1024]{2,1,0:T(8,128)(2,1)}), bf16[32,8,1024]{2,1,0:T(8,128)(2,1)S(1)}, u32[]{:S(2)}, u32[]{:S(2)}) async-start(bf16[32,8,1024]{2,1,0:T(8,128)(2,1)} %stack.2), calls=%async_computation | async-start | bytes 1048576 | tf_op jit(solution)/shard_map/all_to_all | solution.py:119
  193.0 6.4 %copy.94 = bf16[64,8,8,512]{3,2,1,0:T(8,128)(2,1)} copy(bf16[64,8,8,512]{3,1,2,0:T(8,128)(2,1)} %bitcast.464) | data formatting | bytes 8388608
  199.4 7.9 %copy.47 = bf16[8,512,4,128]{3,1,2,0:T(8,128)(2,1)} copy(bf16[8,512,4,128]{1,0,3,2:T(8,128)(2,1)} %bitcast.465) | data formatting | bytes 8388608
  207.3 4.4 copy.95
  215.2 100.0 %while.15 = (s32[]{:T(128)}, f32[4,4,128]{2,1,0:T(4,128)S(1)}, f32[4,4,128]{2,1,0:T(4,128)S(1)}, f32[128,4,4,128]{0,3,2,1:T(8,128)}, s32[8]{0:T(128)S(1)}, /*ind...) while((s32[]{:T(128)}, f32[4,4,128]{2,1,0:T(4,128)S(1)}, ...), condition=%wide.region_3.4_spmd.clone, body=%wide.region_0.3_spmd.clone.sunk | while | flops 551433856 | bytes 33430712 | solution.py:116
  217.9 3.7 fusion.160
  221.6 4.7 fusion.164
  230.1 3.7 fusion.160
  233.9 5.0 %fusion.164 = f32[128,4,4,128]{0,3,2,1:T(8,128)} fusion(f32[4,512,128,4]{2,1,3,0:T(8,128)} %get-tuple-element.251, f32[4,4,128]{2,1,0:T(4,128)S(1)} %get-tuple-element.278, pred[128,512]{0,1:T(8,128)(4,1)S(1)} %compare_and_fusion.2, f32[128,4,4,128]{0,3,2,1:T(8,128)} %get-tuple-element.268, bf16[8,512,4,128]{1,3,2,0:T(8,128)(2,1)} %get-tuple-element.285, ...), kind=kOutput, calls=%fused_computation.9.clone.1 | convolution fusion | flops 274464768 | bytes 6898177 | tf_op jit(solution)/shard_map/while/body/eval_jaxpr/gjtu,ugd->tgjd/dot_general | solution.py:111
  242.6 3.7 fusion.160
  246.4 5.0 %fusion.164 = f32[128,4,4,128]{0,3,2,1:T(8,128)} fusion(f32[4,512,128,4]{2,1,3,0:T(8,128)} %get-tuple-element.251, f32[4,4,128]{2,1,0:T(4,128)S(1)} %get-tuple-element.278, pred[128,512]{0,1:T(8,128)(4,1)S(1)} %compare_and_fusion.2, f32[128,4,4,128]{0,3,2,1:T(8,128)} %get-tuple-element.268, bf16[8,512,4,128]{1,3,2,0:T(8,128)(2,1)} %get-tuple-element.285, ...), kind=kOutput, calls=%fused_computation.9.clone.1 | convolution fusion | flops 274464768 | bytes 6898177 | tf_op jit(solution)/shard_map/while/body/eval_jaxpr/gjtu,ugd->tgjd/dot_general | solution.py:111
  259.0 5.0 %fusion.164 = f32[128,4,4,128]{0,3,2,1:T(8,128)} fusion(f32[4,512,128,4]{2,1,3,0:T(8,128)} %get-tuple-element.251, f32[4,4,128]{2,1,0:T(4,128)S(1)} %get-tuple-element.278, pred[128,512]{0,1:T(8,128)(4,1)S(1)} %compare_and_fusion.2, f32[128,4,4,128]{0,3,2,1:T(8,128)} %get-tuple-element.268, bf16[8,512,4,128]{1,3,2,0:T(8,128)(2,1)} %get-tuple-element.285, ...), kind=kOutput, calls=%fused_computation.9.clone.1 | convolution fusion | flops 274464768 | bytes 6898177 | tf_op jit(solution)/shard_map/while/body/eval_jaxpr/gjtu,ugd->tgjd/dot_general | solution.py:111
  267.7 3.7 fusion.160
  271.5 5.0 %fusion.164 = f32[128,4,4,128]{0,3,2,1:T(8,128)} fusion(f32[4,512,128,4]{2,1,3,0:T(8,128)} %get-tuple-element.251, f32[4,4,128]{2,1,0:T(4,128)S(1)} %get-tuple-element.278, pred[128,512]{0,1:T(8,128)(4,1)S(1)} %compare_and_fusion.2, f32[128,4,4,128]{0,3,2,1:T(8,128)} %get-tuple-element.268, bf16[8,512,4,128]{1,3,2,0:T(8,128)(2,1)} %get-tuple-element.285, ...), kind=kOutput, calls=%fused_computation.9.clone.1 | convolution fusion | flops 274464768 | bytes 6898177 | tf_op jit(solution)/shard_map/while/body/eval_jaxpr/gjtu,ugd->tgjd/dot_general | solution.py:111
  284.0 5.0 %fusion.164 = f32[128,4,4,128]{0,3,2,1:T(8,128)} fusion(f32[4,512,128,4]{2,1,3,0:T(8,128)} %get-tuple-element.251, f32[4,4,128]{2,1,0:T(4,128)S(1)} %get-tuple-element.278, pred[128,512]{0,1:T(8,128)(4,1)S(1)} %compare_and_fusion.2, f32[128,4,4,128]{0,3,2,1:T(8,128)} %get-tuple-element.268, bf16[8,512,4,128]{1,3,2,0:T(8,128)(2,1)} %get-tuple-element.285, ...), kind=kOutput, calls=%fused_computation.9.clone.1 | convolution fusion | flops 274464768 | bytes 6898177 | tf_op jit(solution)/shard_map/while/body/eval_jaxpr/gjtu,ugd->tgjd/dot_general | solution.py:111
  292.8 3.7 fusion.160
  296.6 5.0 %fusion.164 = f32[128,4,4,128]{0,3,2,1:T(8,128)} fusion(f32[4,512,128,4]{2,1,3,0:T(8,128)} %get-tuple-element.251, f32[4,4,128]{2,1,0:T(4,128)S(1)} %get-tuple-element.278, pred[128,512]{0,1:T(8,128)(4,1)S(1)} %compare_and_fusion.2, f32[128,4,4,128]{0,3,2,1:T(8,128)} %get-tuple-element.268, bf16[8,512,4,128]{1,3,2,0:T(8,128)(2,1)} %get-tuple-element.285, ...), kind=kOutput, calls=%fused_computation.9.clone.1 | convolution fusion | flops 274464768 | bytes 6898177 | tf_op jit(solution)/shard_map/while/body/eval_jaxpr/gjtu,ugd->tgjd/dot_general | solution.py:111
  305.3 3.7 fusion.160
  309.1 5.0 %fusion.164 = f32[128,4,4,128]{0,3,2,1:T(8,128)} fusion(f32[4,512,128,4]{2,1,3,0:T(8,128)} %get-tuple-element.251, f32[4,4,128]{2,1,0:T(4,128)S(1)} %get-tuple-element.278, pred[128,512]{0,1:T(8,128)(4,1)S(1)} %compare_and_fusion.2, f32[128,4,4,128]{0,3,2,1:T(8,128)} %get-tuple-element.268, bf16[8,512,4,128]{1,3,2,0:T(8,128)(2,1)} %get-tuple-element.285, ...), kind=kOutput, calls=%fused_computation.9.clone.1 | convolution fusion | flops 274464768 | bytes 6898177 | tf_op jit(solution)/shard_map/while/body/eval_jaxpr/gjtu,ugd->tgjd/dot_general | solution.py:111
  329.3 120.7 %reduce-scatter.2.cloned.1.call-done = f32[8,1024]{1,0:T(8,128)} async-done(((f32[256,1024]{1,0:T(8,128)}), f32[8,1024]{1,0:T(8,128)}) %reduce-scatter.2.cloned.1.call-update) | async-done | bytes 32784 | tf_op jit(solution)/shard_map/reduce_scatter | solution.py:166
  450.0 36.8 %all-gather.1 = f32[128,1024]{1,0:T(8,128)S(1)} all-gather(f32[8,1024]{1,0:T(8,128)} %reduce-scatter.2.cloned.1.call-done), channel_id=3, replica_groups=mesh['seg'=16,'tok'=32] {'seg'}, dimensions={0}, use_global_device_ids=true | all-gather | bytes 557056 | tf_op jit(solution)/shard_map/all_gather | solution.py:167
  (151 shorter events, 74.4 us)
Async XLA Ops:
  7.2 126.0 %copy-start = (bf16[8,512]{1,0:T(8,128)(2,1)S(1)}, bf16[8,512]{1,0:T(8,128)(2,1)}, u32[]{:S(2)}) copy-start(bf16[8,512]{1,0:T(8,128)(2,1)} %param.16) | copy-start | bytes 24580
  7.2 7.8 %copy-start.7 = (s32[16]{0:T(128)S(1)}, s32[16]{0:T(128)}, u32[]{:S(2)}) copy-start(s32[16]{0:T(128)} %param.18) | copy-start | bytes 196
  7.2 9.7 %copy-start.6 = (f32[1,1024]{1,0:T(1,128)S(1)}, f32[1,1024]{1,0:T(1,128)}, u32[]{:S(2)}) copy-start(f32[1,1024]{1,0:T(1,128)} %param.17) | copy-start | bytes 12292
  7.2 120.1 %all-gather.5.cloned.1.call-start = ((), (), s32[]{:S(2)}) async-start(), calls=%async_computation.2 | async-start | bytes 8650752 | tf_op jit(solution)/shard_map/all_gather | solution.py:45
  136.3 3.5 copy-start.2
  136.3 4.8 copy-start.5
  183.8 131.3 %all-to-all-start = ((bf16[32,8,1024]{2,1,0:T(8,128)(2,1)}), bf16[32,8,1024]{2,1,0:T(8,128)(2,1)S(1)}, u32[]{:S(2)}, u32[]{:S(2)}) async-start(bf16[32,8,1024]{2,1,0:T(8,128)(2,1)} %stack.2), calls=%async_computation | async-start | bytes 1048576 | tf_op jit(solution)/shard_map/all_to_all | solution.py:119
  193.0 257.0 %reduce-scatter.2.cloned.1.call-start = ((), (), s32[]{:S(2)}) async-start(), calls=%async_computation.3 | async-start | bytes 1081344 | tf_op jit(solution)/shard_map/reduce_scatter | solution.py:166
  221.6 4.7 copy-start.1
  233.9 5.0 %copy-start.1 = (f32[4,512,128,4]{2,1,3,0:T(8,128)S(1)}, f32[4,512,128,4]{2,1,3,0:T(8,128)}, u32[]{:S(2)}) copy-start(f32[4,512,128,4]{2,1,3,0:T(8,128)} %get-tuple-element.251) | copy-start | bytes 12582916 | tf_op jit(solution)/shard_map/while
  246.4 5.0 %copy-start.1 = (f32[4,512,128,4]{2,1,3,0:T(8,128)S(1)}, f32[4,512,128,4]{2,1,3,0:T(8,128)}, u32[]{:S(2)}) copy-start(f32[4,512,128,4]{2,1,3,0:T(8,128)} %get-tuple-element.251) | copy-start | bytes 12582916 | tf_op jit(solution)/shard_map/while
  258.9 5.0 %copy-start.1 = (f32[4,512,128,4]{2,1,3,0:T(8,128)S(1)}, f32[4,512,128,4]{2,1,3,0:T(8,128)}, u32[]{:S(2)}) copy-start(f32[4,512,128,4]{2,1,3,0:T(8,128)} %get-tuple-element.251) | copy-start | bytes 12582916 | tf_op jit(solution)/shard_map/while
  271.5 5.0 %copy-start.1 = (f32[4,512,128,4]{2,1,3,0:T(8,128)S(1)}, f32[4,512,128,4]{2,1,3,0:T(8,128)}, u32[]{:S(2)}) copy-start(f32[4,512,128,4]{2,1,3,0:T(8,128)} %get-tuple-element.251) | copy-start | bytes 12582916 | tf_op jit(solution)/shard_map/while
  284.0 5.0 %copy-start.1 = (f32[4,512,128,4]{2,1,3,0:T(8,128)S(1)}, f32[4,512,128,4]{2,1,3,0:T(8,128)}, u32[]{:S(2)}) copy-start(f32[4,512,128,4]{2,1,3,0:T(8,128)} %get-tuple-element.251) | copy-start | bytes 12582916 | tf_op jit(solution)/shard_map/while
  296.6 5.0 %copy-start.1 = (f32[4,512,128,4]{2,1,3,0:T(8,128)S(1)}, f32[4,512,128,4]{2,1,3,0:T(8,128)}, u32[]{:S(2)}) copy-start(f32[4,512,128,4]{2,1,3,0:T(8,128)} %get-tuple-element.251) | copy-start | bytes 12582916 | tf_op jit(solution)/shard_map/while
  309.1 5.0 %copy-start.1 = (f32[4,512,128,4]{2,1,3,0:T(8,128)S(1)}, f32[4,512,128,4]{2,1,3,0:T(8,128)}, u32[]{:S(2)}) copy-start(f32[4,512,128,4]{2,1,3,0:T(8,128)} %get-tuple-element.251) | copy-start | bytes 12582916 | tf_op jit(solution)/shard_map/while
  318.7 4.2 copy-start.4
  324.6 3.7 copy-start.3
Sparse Core Ops, SparseCore 0:
  11.7 115.5 all-gather.4
  328.4 121.6 reduce-scatter.1
